TPU v7x, 256 devices: a whole 4x4x8 slice. The times are simulated.
256 devices in a mesh: dp: 32 (over z, x), mp: 8 (over y, core).
Axes of the slice: x: 4, y: 4, z: 8, core: 2. Of those that a mesh axis runs over, the one named last changes fastest.
Arguments:
- token_ids: int32 [2048, 7], replicated, may hold values from 0 to 65535
- lengths: int32 [2048], replicated, may hold values from 1 to 7, as said below
- pack_dest: int32 [2048], replicated, may hold values from 0 to 31, as said below
- ref_hidden: bfloat16 [2048, 7, 4096], P('dp', None, 'mp'), may hold values from -45 to 45
- reward_hidden: bfloat16 [2048, 7, 4096], P('dp', None, 'mp'), may hold values from -140 to 140
- head_weight: bfloat16 [4096, 65536], P('mp', 'dp'), may hold values from -0.25 to 0.25
- norm_gain: float32 [4096], P('mp'), may hold values from 0.1 to 1.9
- score_weight: float32 [4096], P('mp'), may hold values from -0.09375 to 0.09375
- value_weight: float32 [4096], P('mp'), may hold values from -0.09375 to 0.09375
- old_logprob: float32 [8192], P('dp'), may hold values from -14 to -1
Outputs:
- ref_logprob: float32 [8192], P('dp')
- advantage: float32 [8192], P('dp')
Inputs may be any that keep to these rules, and one draw needn't show every extreme that they name: `pack_dest`: request i belongs to request shard i // 64. Each request shard sends exactly 2 of its requests to every packed shard. A packed shard lists its requests by request shard, then by request index, and packs their tokens in that order from slot 0. In that order the requests of a packed shard form pairs whose lengths sum to 8, so every packed shard holds exactly 256 tokens; every packed shard has a request of length 1 and one of length 7.
All inputs are finite; a program needn't handle non-finite values.
Results may differ from a plain program's by a relative error of at most 0.0003.
Values may be sent and summed in bfloat16 or wider, within the bound.
No kernel may reach another device: no remote copies, remote signals or barrier semaphores. Data moves between devices by JAX's collectives and lax.ppermute only.
A program may use at most 192 MiB of HBM per device.

v0:
```python
import jax
import jax.numpy as jnp
from jax import lax
from jax.sharding import PartitionSpec as P

kl_coef = 0.1
discount = 0.99
gae_mix = 0.95
norm_eps = 1e-05


def pair_rank(dest):
    count = dest.shape[-1]
    idx = jnp.arange(count, dtype=jnp.int32)
    same = dest[..., None, :] == dest[..., :, None]
    earlier = idx[None, :] < idx[:, None]
    return jnp.sum(jnp.logical_and(same, earlier).astype(jnp.int32), axis=-1)


def body(
    token_ids,
    lengths,
    pack_dest,
    ref_hidden,
    reward_hidden,
    head_weight,
    norm_gain,
    score_weight,
    value_weight,
    old_logprob,
):
    shards = lax.axis_size("dp")
    ways = lax.axis_size("mp")
    me = lax.axis_index("dp")
    part = lax.axis_index("mp")
    req_dev, max_len, width_dev = ref_hidden.shape
    pair_len = max_len + 1
    slot_dev = shards * pair_len
    sub_len = slot_dev // ways
    blocks = sub_len // pair_len
    width_full = width_dev * ways
    steps = jnp.arange(max_len, dtype=jnp.int32)
    dest = lax.dynamic_slice_in_dim(pack_dest, me * req_dev, req_dev)
    size = lax.dynamic_slice_in_dim(lengths, me * req_dev, req_dev)
    rank = pair_rank(dest)
    row = dest[:, None] * pair_len + steps[None, :] + rank[:, None] * (pair_len - size[:, None])
    row = jnp.where(steps[None, :] < size[:, None], row, -1).reshape(-1)
    onehot = (row[None, :] == jnp.arange(slot_dev, dtype=jnp.int32)[:, None]).astype(jnp.bfloat16)
    ref_send = jnp.dot(
        onehot, ref_hidden.reshape(req_dev * max_len, width_dev), preferred_element_type=jnp.float32
    ).astype(jnp.bfloat16)
    reward_send = jnp.dot(
        onehot,
        reward_hidden.reshape(req_dev * max_len, width_dev),
        preferred_element_type=jnp.float32,
    ).astype(jnp.bfloat16)
    send = jnp.concatenate([ref_send, reward_send], axis=1).reshape(shards, pair_len, 2 * width_dev)
    got = lax.all_to_all(send, "dp", 0, 0, tiled=True).reshape(slot_dev, 2 * width_dev)
    ref_packed = got[:, :width_dev]
    reward_packed = got[:, width_dev:]
    own_rows = lax.all_to_all(
        ref_packed.reshape(ways, sub_len, width_dev), "mp", 0, 2, tiled=True
    ).reshape(sub_len, width_full)
    block_rows = lax.all_gather(own_rows, "dp", axis=0, tiled=True)
    weight = lax.all_gather(head_weight, "mp", axis=0, tiled=True)
    first_src = part * blocks
    dest4 = lax.dynamic_slice_in_dim(pack_dest, first_src * req_dev, blocks * req_dev).reshape(
        blocks, req_dev
    )
    size4 = lax.dynamic_slice_in_dim(lengths, first_src * req_dev, blocks * req_dev).reshape(
        blocks, req_dev
    )
    tok4 = lax.dynamic_slice_in_dim(token_ids, first_src * req_dev, blocks * req_dev, axis=0)
    rank4 = pair_rank(dest4)
    key = (
        dest4[:, :, None] * sub_len
        + jnp.arange(blocks, dtype=jnp.int32)[:, None, None] * pair_len
        + steps[None, None, :]
        + rank4[:, :, None] * (pair_len - size4[:, :, None])
    )
    key = jnp.where(steps[None, None, :] < size4[:, :, None], key, -1).reshape(-1)
    hits = key[None, :] == jnp.arange(shards * sub_len, dtype=jnp.int32)[:, None]
    targets = jnp.sum(jnp.where(hits, tok4.reshape(-1)[None, :], 0), axis=1)
    logits = jnp.dot(block_rows, weight, preferred_element_type=jnp.float32)
    vocab_dev = head_weight.shape[1]
    row_max = jnp.max(logits, axis=1)
    exp_total = jnp.sum(jnp.exp(logits - row_max[:, None]), axis=1)
    column = jnp.arange(vocab_dev, dtype=jnp.int32)[None, :] + me * vocab_dev
    target_logit = jnp.sum(jnp.where(column == targets[:, None], logits, 0.0), axis=1)
    stats = jnp.stack([row_max, exp_total, target_logit]).reshape(3, shards, sub_len)
    stats = lax.all_to_all(stats, "dp", 1, 1, tiled=True)
    joint_max = jnp.max(stats[0], axis=0)
    joint_total = jnp.sum(stats[1] * jnp.exp(stats[0] - joint_max[None, :]), axis=0)
    joint_target = jnp.sum(stats[2], axis=0)
    block_logprob = joint_target - joint_max - jnp.log(joint_total)
    ref_logprob = lax.all_gather(block_logprob, "mp", axis=0, tiled=True)
    hidden_f = reward_packed.astype(jnp.float32)
    sums = jnp.stack(
        [
            jnp.sum(hidden_f * hidden_f, axis=1),
            jnp.sum(hidden_f * (norm_gain * score_weight), axis=1),
            jnp.sum(hidden_f * (norm_gain * value_weight), axis=1),
        ]
    )
    squares, score_dot, value_dot = lax.psum(sums, "mp")
    inv_rms = lax.rsqrt(squares / width_full + norm_eps)
    score = score_dot * inv_rms
    value_est = value_dot * inv_rms
    mine = (pack_dest.reshape(shards, req_dev) == me).astype(jnp.int32)
    is_first = jnp.logical_and(mine == 1, jnp.cumsum(mine, axis=1) == 1)
    first_len = jnp.sum(jnp.where(is_first, lengths.reshape(shards, req_dev), 0), axis=1)
    place = jnp.arange(pair_len, dtype=jnp.int32)[None, :]
    is_last = jnp.logical_or(place == first_len[:, None] - 1, place == pair_len - 1)
    is_last_flat = is_last.reshape(-1)
    reward = -kl_coef * (old_logprob - ref_logprob) + jnp.where(is_last_flat, score, 0.0)
    next_value = jnp.concatenate([value_est[1:], jnp.zeros((1,), jnp.float32)])
    not_last = 1.0 - is_last_flat.astype(jnp.float32)
    td_error = (reward + discount * next_value * not_last - value_est).reshape(shards, pair_len)
    decay = discount * gae_mix
    carry = td_error[:, pair_len - 1]
    columns = [carry]
    for step in range(pair_len - 2, -1, -1):
        carry = td_error[:, step] + decay * jnp.where(is_last[:, step], 0.0, carry)
        columns.append(carry)
    advantage = jnp.stack(columns[::-1], axis=1).reshape(-1)
    return (ref_logprob, advantage)


def solution(mesh):
    return jax.shard_map(
        body,
        mesh=mesh,
        in_specs=(
            P(),
            P(),
            P(),
            P("dp", None, "mp"),
            P("dp", None, "mp"),
            P("mp", "dp"),
            P("mp"),
            P("mp"),
            P("mp"),
            P("dp"),
        ),
        out_specs=(P("dp"), P("dp")),
        check_vma=False,
    )
```

profile of v0, /device:TPU:1, one launch (start us, length us, event | category | flops | bytes accessed | tf_op | source)
XLA Modules:
  0.0 304.3 jit_solution(12371459190618607233)
XLA Ops:
  7.3 0.8 broadcast_multiply_fusion
  8.1 0.2 convert_reduce_fusion.1
  8.2 0.8 subtract_multiply_fusion.1
  9.1 0.1 select_n.99
  9.3 1.3 copy.33
  10.5 0.2 reshape.220
  10.7 1.3 copy.34
  12.0 0.2 reshape.221
  12.2 0.3 convolution_convert_fusion.1
  12.5 0.3 convolution_convert_fusion
  12.9 27.9 %all_to_all.25 = bf16[32,8,1024]{2,1,0:T(8,128)(2,1)S(1)} all-to-all(bf16[32,8,1024]{2,1,0:T(8,128)(2,1)S(1)} %maximum_bitcast_fusion), channel_id=1, replica_groups=mesh['dp'=32,'mp'=8] {'dp'}, dimensions={0} | all-to-all | bytes 1048576 | tf_op jit(solution)/shard_map/all_to_all | solution.py:58
  40.8 13.2 %all_to_all.26 = bf16[8,32,512]{2,1,0:T(8,128)(2,1)S(1)} all-to-all(bf16[8,32,512]{2,1,0:T(8,128)(2,1)S(1)} %bitcast.31), channel_id=1, replica_groups=mesh['dp'=32,'mp'=8] {'mp'}, dimensions={0} | all-to-all | bytes 524288 | tf_op jit(solution)/shard_map/all_to_all | solution.py:61
  54.0 0.7 copy.39
  54.8 0.7 all-gather.5.cloned.1.call-update
  56.0 0.2 reduce_window_sum.11
  56.7 0.2 broadcast_in_dim.45
  56.9 0.2 convert_reduce_fusion
  57.2 0.2 add_select_fusion
  57.4 0.2 select_n.102
  57.6 0.6 dynamic-slice
  58.9 0.8 select_reduce_fusion.1
  59.7 0.2 fusion
  59.9 86.8 %all-gather.3.cloned.1.call-done = bf16[1024,4096]{1,0:T(8,128)(2,1)} async-done(((bf16[32,4096]{1,0:T(8,128)(2,1)}), bf16[1024,4096]{1,0:T(8,128)(2,1)}) %all-gather.3.cloned.1.call-update) | async-done | bytes 8388624 | tf_op jit(solution)/shard_map/all_gather | solution.py:64
  146.7 87.6 %all-gather.5.cloned.1.call-done = bf16[4096,2048]{1,0:T(8,128)(2,1)} async-done(((bf16[512,2048]{1,0:T(8,128)(2,1)}), bf16[4096,2048]{1,0:T(8,128)(2,1)}) %all-gather.5.cloned.1.call-update) | async-done | bytes 16777232 | tf_op jit(solution)/shard_map/all_gather | solution.py:65
  234.3 24.2 %fusion.12 = (f32[1024]{0:T(1024)S(1)}, f32[1024,2048]{1,0:T(8,128)}) fusion(bf16[1024,4096]{1,0:T(8,128)(2,1)} %all-gather.3.cloned.1.call-done, bf16[4096,2048]{1,0:T(8,128)(2,1)} %all-gather.5.cloned.1.call-done), kind=kOutput, calls=%fused_computation.58 | convolution fusion | flops 17181966336 | bytes 33558528 | tf_op jit(solution)/shard_map/dot_general | solution.py:84
  258.6 4.7 %exponential_reduce_fusion = (f32[1024]{0:T(1024)S(1)}, f32[1024]{0:T(1024)S(1)}) fusion(f32[1024,2048]{1,0:T(8,128)} %get-tuple-element.29, f32[1024]{0:T(1024)S(1)} %get-tuple-element.28, s32[1024]{0:T(1024)S(1)} %select_reduce_fusion.1, s32[2048]{0:T(1024)S(1)} %iota_add_fusion), kind=kLoop, calls=%fused_computation.1 | loop fusion | flops 10483712 | bytes 8413184 | tf_op jit(solution)/shard_map/reduce_sum | solution.py:87
  263.4 0.7 pad_maximum_fusion
  264.1 9.5 %all-to-all-start.2 = ((f32[3,32,32]{2,0,1:T(4,128)}), f32[3,32,32]{2,0,1:T(4,128)S(1)}, u32[]{:S(2)}, u32[]{:S(2)}) async-start(f32[3,32,32]{2,0,1:T(4,128)} %pad_maximum_fusion), calls=%async_computation.2 | async-start | bytes 131072 | tf_op jit(solution)/shard_map/all_to_all | solution.py:91
  273.6 8.9 %all-to-all-done.2 = f32[3,32,32]{2,0,1:T(4,128)S(1)} async-done(((f32[3,32,32]{2,0,1:T(4,128)}), f32[3,32,32]{2,0,1:T(4,128)S(1)}, u32[]{:S(2)}, u32[]{:S(2)}) %all-to-all-start.2) | async-done | bytes 12320 | tf_op jit(solution)/shard_map/all_to_all | solution.py:91
  282.7 13.6 %all-reduce.1 = (f32[256]{0:T(256)S(1)}, f32[3,256]{1,0:T(4,128)S(1)}) all-reduce(f32[256]{0:T(256)S(1)} %subtract_dynamic-update-slice_fusion, f32[3,256]{1,0:T(4,128)S(1)} %pad_maximum_fusion.1), channel_id=1, replica_groups=mesh['dp'=32,'mp'=8] {'mp'}, use_global_device_ids=true, to_apply=%add | all-reduce | flops 1024 | bytes 8192
  296.6 0.1 slice_add_fusion.6
  296.8 0.7 reshape.228
  (57 shorter events, 2.1 us)
Async XLA Ops:
  7.2 49.3 %copy-start = (s32[2048,7]{0,1:T(8,128)S(1)}, s32[2048,7]{0,1:T(8,128)}, u32[]{:S(2)}) copy-start(s32[2048,7]{0,1:T(8,128)} %param.10) | copy-start | bytes 172036
  7.2 50.4 %copy-start.8 = (u32[256]{0:T(256)S(1)}, u32[256]{0:T(256)}, u32[]{:S(2)}) copy-start(u32[256]{0:T(256)} %constant.56) | copy-start | bytes 3076
  7.2 48.4 %copy-start.2 = (s32[2048]{0:T(1024)S(1)}, s32[2048]{0:T(1024)}, u32[]{:S(2)}) copy-start(s32[2048]{0:T(1024)} %param.12) | copy-start | bytes 24580
  7.2 48.3 %copy-start.1 = (s32[2048]{0:T(1024)S(1)}, s32[2048]{0:T(1024)}, u32[]{:S(2)}) copy-start(s32[2048]{0:T(1024)} %param.11) | copy-start | bytes 24580
  7.2 51.6 %copy-start.5 = (f32[512]{0:T(512)S(1)}, f32[512]{0:T(512)}, u32[]{:S(2)}) copy-start(f32[512]{0:T(512)} %param.18) | copy-start | bytes 6148
  7.2 51.6 %copy-start.4 = (f32[512]{0:T(512)S(1)}, f32[512]{0:T(512)}, u32[]{:S(2)}) copy-start(f32[512]{0:T(512)} %param.17) | copy-start | bytes 6148
  7.2 51.6 %copy-start.3 = (f32[512]{0:T(512)S(1)}, f32[512]{0:T(512)}, u32[]{:S(2)}) copy-start(f32[512]{0:T(512)} %param.16) | copy-start | bytes 6148
  7.2 139.5 %all-gather.3.cloned.1.call-start = ((), (), s32[]{:S(2)}) async-start(), calls=%async_computation.3 | async-start | bytes 8650752 | tf_op jit(solution)/shard_map/all_gather | solution.py:64
  54.7 179.6 %all-gather.5.cloned.1.call-start = ((), (), s32[]{:S(2)}) async-start(), calls=%async_computation.4 | async-start | bytes 18874368 | tf_op jit(solution)/shard_map/all_gather | solution.py:65
  258.5 37.9 %copy-start.6 = (f32[256]{0:T(256)S(1)}, f32[256]{0:T(256)}, u32[]{:S(2)}) copy-start(f32[256]{0:T(256)} %param.19) | copy-start | bytes 3076
  264.1 18.4 %all-to-all-start.2 = ((f32[3,32,32]{2,0,1:T(4,128)}), f32[3,32,32]{2,0,1:T(4,128)S(1)}, u32[]{:S(2)}, u32[]{:S(2)}) async-start(f32[3,32,32]{2,0,1:T(4,128)} %pad_maximum_fusion), calls=%async_computation.2 | async-start | bytes 131072 | tf_op jit(solution)/shard_map/all_to_all | solution.py:91
  296.3 1.2 copy-start.7
Sparse Core Ops, SparseCore 0:
  54.8 91.8 all-gather.2
  148.6 85.6 all-gather.4
where the time goes:
time: 305 us; the launch traced here: 304 us
  waiting for transfers between devices  184 us (60%)
  blocking collectives  54.7 us (18%)
  matrix products  24.8 us (8%)
  between operations  15 us (5%)
  starting transfers between devices  9.61 us (3%)
  other arithmetic  9.59 us (3%)
  local copies, waits for them, and re-layouts  6.68 us (2%)
    all_gather x1, waiting for transfers between devices, body(): weight = lax.all_gather(head_weight, 'mp', axis=0, tiled=True)  87.6 us
    all_gather x1, waiting for transfers between devices, body(): block_rows = lax.all_gather(own_rows, 'dp', axis=0, tiled=True)  86.8 us
    all_to_all x1, blocking collectives, body(): lax.all_to_all(send, 'dp', 0, 0, tiled=True)  27.9 us
    dot_general x1, matrix products, body(): logits = jnp.dot(block_rows, weight, preferred_element_type=jnp.float32)  24.2 us
    unnamed x1, blocking collectives  13.6 us
    all_to_all x1, blocking collectives, body(): lax.all_to_all(ref_packed.reshape(ways, sub_len, width_dev), 'mp', 0, 2,...  13.2 us
    all_to_all x1, starting transfers between devices, body(): stats = lax.all_to_all(stats, 'dp', 1, 1, tiled=True)  9.53 us
    all_to_all x1, waiting for transfers between devices, body(): stats = lax.all_to_all(stats, 'dp', 1, 1, tiled=True)  8.86 us
  transfers between devices with their start and end apart: 3, of which 3 were waited for; matrix products, arithmetic and copies ran while one was open for 1% of the time, Pallas kernels for 0%

commit v1 on v0

--- a/solution.py
+++ b/solution.py
@@ -7,6 +7,13 @@
 discount = 0.99
 gae_mix = 0.95
 norm_eps = 1e-05
+
+
+def all_by_exchange(shard, axis, d):
+    size = lax.axis_size(axis)
+    shards = jnp.stack([shard for _ in range(size)])
+    shards = lax.all_to_all(shards, axis, split_axis=0, concat_axis=0)
+    return jnp.concatenate(shards, axis=d)
 
 
 def pair_rank(dest):
@@ -62,7 +69,7 @@
         ref_packed.reshape(ways, sub_len, width_dev), "mp", 0, 2, tiled=True
     ).reshape(sub_len, width_full)
     block_rows = lax.all_gather(own_rows, "dp", axis=0, tiled=True)
-    weight = lax.all_gather(head_weight, "mp", axis=0, tiled=True)
+    weight = all_by_exchange(head_weight, "mp", 0)
     first_src = part * blocks
     dest4 = lax.dynamic_slice_in_dim(pack_dest, first_src * req_dev, blocks * req_dev).reshape(
         blocks, req_dev

time: 305 us -> 319 us (1.046)
  local copies, waits for them, and re-layouts: 6.68 us -> 13.4 us
  waiting for transfers between devices: 184 us -> 188 us
    all_to_all x0 -> x1, waiting for transfers between devices: none -> 179 us  [all_by_exchange(): shards = lax.all_to_all(shards, axis, split_axis=0, concat_axis=0)]
    all_gather x1 -> x0, waiting for transfers between devices: 87.6 us -> none  [body(): weight = lax.all_gather(head_weight, 'mp', axis=0, tiled=True)]
    all_gather x1, waiting for transfers between devices: 86.8 us -> 0.01 us  [body(): block_rows = lax.all_gather(own_rows, 'dp', axis=0, tiled=True)]
    all_to_all x0 -> x1, starting transfers between devices: none -> 6.81 us  [all_by_exchange(): shards = lax.all_to_all(shards, axis, split_axis=0, concat_axis=0)]
    another operation x0 -> x1, local copies, waits for them, and re-layouts: none -> 5.98 us  [all_by_exchange(): shards = jnp.stack([shard for _ in range(size)])]
    all_to_all x1, starting transfers between devices: 9.53 us -> 4.35 us  [body(): stats = lax.all_to_all(stats, 'dp', 1, 1, tiled=True)]
  transfers between devices with their start and end apart: 3 -> 3, of which waited for: 3 -> 2; matrix products, arithmetic and copies ran while one was open for 1% -> 3% of each run, Pallas kernels for 0% -> 0%
where the time goes in v1:
time: 319 us
  waiting for transfers between devices  188 us (59%)
  blocking collectives  55.4 us (17%)
  matrix products  25.9 us (8%)
  between operations  15 us (5%)
  local copies, waits for them, and re-layouts  13.4 us (4%)
  starting transfers between devices  11.2 us (4%)
  other arithmetic  9.72 us (3%)
    all_to_all x1, waiting for transfers between devices, all_by_exchange(): shards = lax.all_to_all(shards, axis, split_axis=0, concat_axis=0)  179 us
    all_to_all x1, blocking collectives, body(): lax.all_to_all(send, 'dp', 0, 0, tiled=True)  27.9 us
    dot_general x1, matrix products, body(): logits = jnp.dot(block_rows, weight, preferred_element_type=jnp.float32)  24.2 us
    unnamed x1, blocking collectives  14.3 us
    all_to_all x1, blocking collectives, body(): lax.all_to_all(ref_packed.reshape(ways, sub_len, width_dev), 'mp', 0, 2,...  13.2 us
    all_to_all x1, waiting for transfers between devices, body(): stats = lax.all_to_all(stats, 'dp', 1, 1, tiled=True)  8.82 us
    all_to_all x1, starting transfers between devices, all_by_exchange(): shards = lax.all_to_all(shards, axis, split_axis=0, concat_axis=0)  6.81 us
  transfers between devices with their start and end apart: 3, of which 2 were waited for; matrix products, arithmetic and copies ran while one was open for 3% of the time, Pallas kernels for 0%

profile of v1, /device:TPU:1, one launch (start us, length us, event | category | flops | bytes accessed | tf_op | source)
XLA Modules:
  0.0 318.6 jit_solution(14062374751175661631)
XLA Ops:
  7.2 0.9 broadcast_multiply_fusion
  8.1 0.2 convert_reduce_fusion.1
  8.3 0.8 subtract_multiply_fusion.1
  9.2 0.1 select_n.99
  9.3 1.3 copy.33
  10.6 0.2 reshape.225
  10.8 1.3 copy.34
  12.1 0.9 reshape.226
  13.0 0.3 convolution_convert_fusion.1
  13.3 1.3 convolution_convert_fusion
  14.7 27.9 %all_to_all.30 = bf16[32,8,1024]{2,1,0:T(8,128)(2,1)S(1)} all-to-all(bf16[32,8,1024]{2,1,0:T(8,128)(2,1)S(1)} %maximum_bitcast_fusion), channel_id=1, replica_groups=mesh['dp'=32,'mp'=8] {'dp'}, dimensions={0} | all-to-all | bytes 1048576 | tf_op jit(solution)/shard_map/all_to_all | solution.py:65
  42.7 13.2 %all_to_all.31 = bf16[8,32,512]{2,1,0:T(8,128)(2,1)S(1)} all-to-all(bf16[8,32,512]{2,1,0:T(8,128)(2,1)S(1)} %bitcast.32), channel_id=1, replica_groups=mesh['dp'=32,'mp'=8] {'mp'}, dimensions={0} | all-to-all | bytes 524288 | tf_op jit(solution)/shard_map/all_to_all | solution.py:68
  55.8 0.7 copy.39
  56.6 6.0 %stack.20 = bf16[8,512,2048]{2,1,0:T(8,128)(2,1)} broadcast(bf16[512,2048]{1,0:T(8,128)(2,1)S(1)} %copy-done.1), dimensions={1,2} | broadcast | bytes 18874368 | tf_op jit(solution)/shard_map/stack | solution.py:14
  62.6 6.8 %all-to-all-start.2 = ((bf16[8,512,2048]{2,1,0:T(8,128)(2,1)}), bf16[8,512,2048]{2,1,0:T(8,128)(2,1)}, u32[]{:S(2)}, u32[]{:S(2)}) async-start(bf16[8,512,2048]{2,1,0:T(8,128)(2,1)} %stack.20), calls=%async_computation.2 | async-start | bytes 33554432 | tf_op jit(solution)/shard_map/all_to_all | solution.py:15
  69.9 0.2 reduce_window_sum.11
  70.6 0.2 broadcast_in_dim.45
  70.8 0.2 convert_reduce_fusion
  71.1 0.2 add_select_fusion
  71.3 0.2 select_n.102
  71.5 0.6 dynamic-slice
  72.8 0.8 select_reduce_fusion.1
  73.6 0.2 fusion
  73.8 179.2 %all-to-all-done.2 = bf16[8,512,2048]{2,1,0:T(8,128)(2,1)} async-done(((bf16[8,512,2048]{2,1,0:T(8,128)(2,1)}), bf16[8,512,2048]{2,1,0:T(8,128)(2,1)}, u32[]{:S(2)}, u32[]{:S(2)}) %all-to-all-start.2) | async-done | bytes 16777248 | tf_op jit(solution)/shard_map/all_to_all | solution.py:15
  253.1 24.2 %fusion.12 = (f32[1024]{0:T(1024)S(1)}, f32[1024,2048]{1,0:T(8,128)}) fusion(bf16[1024,4096]{1,0:T(8,128)(2,1)} %all-gather.2.cloned.1.call-done, bf16[4096,2048]{1,0:T(8,128)(2,1)} %bitcast.5), kind=kOutput, calls=%fused_computation.58 | convolution fusion | flops 17181966336 | bytes 33558528 | tf_op jit(solution)/shard_map/dot_general | solution.py:91
  277.4 4.6 %exponential_reduce_fusion = (f32[1024]{0:T(1024)S(1)}, f32[1024]{0:T(1024)S(1)}) fusion(f32[1024,2048]{1,0:T(8,128)} %get-tuple-element.29, f32[1024]{0:T(1024)S(1)} %get-tuple-element.28, s32[1024]{0:T(1024)S(1)} %select_reduce_fusion.1, s32[2048]{0:T(1024)S(1)} %iota_add_fusion), kind=kLoop, calls=%fused_computation.1 | loop fusion | flops 10483712 | bytes 8413184 | tf_op jit(solution)/shard_map/reduce_sum | solution.py:94
  282.2 0.7 pad_maximum_fusion
  282.9 4.3 %all-to-all-start.3 = ((f32[3,32,32]{2,0,1:T(4,128)}), f32[3,32,32]{2,0,1:T(4,128)S(1)}, u32[]{:S(2)}, u32[]{:S(2)}) async-start(f32[3,32,32]{2,0,1:T(4,128)} %pad_maximum_fusion), calls=%async_computation.3 | async-start | bytes 131072 | tf_op jit(solution)/shard_map/all_to_all | solution.py:98
  287.2 8.8 %all-to-all-done.3 = f32[3,32,32]{2,0,1:T(4,128)S(1)} async-done(((f32[3,32,32]{2,0,1:T(4,128)}), f32[3,32,32]{2,0,1:T(4,128)S(1)}, u32[]{:S(2)}, u32[]{:S(2)}) %all-to-all-start.3) | async-done | bytes 12320 | tf_op jit(solution)/shard_map/all_to_all | solution.py:98
  296.3 14.3 %all-reduce.1 = (f32[256]{0:T(256)S(1)}, f32[3,256]{1,0:T(4,128)S(1)}) all-reduce(f32[256]{0:T(256)S(1)} %subtract_dynamic-update-slice_fusion, f32[3,256]{1,0:T(4,128)S(1)} %pad_maximum_fusion.1), channel_id=1, replica_groups=mesh['dp'=32,'mp'=8] {'mp'}, use_global_device_ids=true, to_apply=%add | all-reduce | flops 1024 | bytes 8192
  310.9 0.1 slice_add_fusion.6
  311.1 0.7 reshape.234
  (59 shorter events, 2.1 us)
Async XLA Ops:
  7.2 63.3 %copy-start = (s32[2048,7]{0,1:T(8,128)S(1)}, s32[2048,7]{0,1:T(8,128)}, u32[]{:S(2)}) copy-start(s32[2048,7]{0,1:T(8,128)} %param.10) | copy-start | bytes 172036
  7.2 49.4 %copy-start.1 = (bf16[512,2048]{1,0:T(8,128)(2,1)S(1)}, bf16[512,2048]{1,0:T(8,128)(2,1)}, u32[]{:S(2)}) copy-start(bf16[512,2048]{1,0:T(8,128)(2,1)} %param.15) | copy-start | bytes 6291460
  7.2 245.9 %all-gather.2.cloned.1.call-start = ((), (), s32[]{:S(2)}) async-start(), calls=%async_computation.4 | async-start | bytes 8650752 | tf_op jit(solution)/shard_map/all_gather | solution.py:71
  62.6 6.9 %copy-start.2 = (s32[2048]{0:T(1024)S(1)}, s32[2048]{0:T(1024)}, u32[]{:S(2)}) copy-start(s32[2048]{0:T(1024)} %param.11) | copy-start | bytes 24580
  62.6 6.9 %copy-start.3 = (s32[2048]{0:T(1024)S(1)}, s32[2048]{0:T(1024)}, u32[]{:S(2)}) copy-start(s32[2048]{0:T(1024)} %param.12) | copy-start | bytes 24580
  62.6 9.0 %copy-start.9 = (u32[256]{0:T(256)S(1)}, u32[256]{0:T(256)}, u32[]{:S(2)}) copy-start(u32[256]{0:T(256)} %constant.56) | copy-start | bytes 3076
  62.6 10.2 %copy-start.4 = (f32[512]{0:T(512)S(1)}, f32[512]{0:T(512)}, u32[]{:S(2)}) copy-start(f32[512]{0:T(512)} %param.16) | copy-start | bytes 6148
  62.6 10.2 %copy-start.5 = (f32[512]{0:T(512)S(1)}, f32[512]{0:T(512)}, u32[]{:S(2)}) copy-start(f32[512]{0:T(512)} %param.17) | copy-start | bytes 6148
  62.6 10.2 %copy-start.6 = (f32[512]{0:T(512)S(1)}, f32[512]{0:T(512)}, u32[]{:S(2)}) copy-start(f32[512]{0:T(512)} %param.18) | copy-start | bytes 6148
  62.6 190.4 %all-to-all-start.2 = ((bf16[8,512,2048]{2,1,0:T(8,128)(2,1)}), bf16[8,512,2048]{2,1,0:T(8,128)(2,1)}, u32[]{:S(2)}, u32[]{:S(2)}) async-start(bf16[8,512,2048]{2,1,0:T(8,128)(2,1)} %stack.20), calls=%async_computation.2 | async-start | bytes 33554432 | tf_op jit(solution)/shard_map/all_to_all | solution.py:15
  277.3 33.4 %copy-start.7 = (f32[256]{0:T(256)S(1)}, f32[256]{0:T(256)}, u32[]{:S(2)}) copy-start(f32[256]{0:T(256)} %param.19) | copy-start | bytes 3076
  282.9 13.2 %all-to-all-start.3 = ((f32[3,32,32]{2,0,1:T(4,128)}), f32[3,32,32]{2,0,1:T(4,128)S(1)}, u32[]{:S(2)}, u32[]{:S(2)}) async-start(f32[3,32,32]{2,0,1:T(4,128)} %pad_maximum_fusion), calls=%async_computation.3 | async-start | bytes 131072 | tf_op jit(solution)/shard_map/all_to_all | solution.py:98
  310.6 1.2 copy-start.8
Sparse Core Ops, SparseCore 0:
  56.7 91.7 all-gather.1
